TPU v7x, 512 devices: a whole 4x8x8 slice. The times are simulated.
512 devices in a mesh: ctx: 64 (over y, x, core), head: 8 (over z).
Axes of the slice: x: 4, y: 8, z: 8, core: 2. Of those that a mesh axis runs over, the one named last changes fastest.
Arguments:
- tokens: bfloat16 [65536, 2048], P('ctx', 'head'), may hold values from -6 to 6
- w_qkv: bfloat16 [3, 2048, 2048], P(None, 'ctx', 'head'), may hold values from -0.125 to 0.125
- out_gain: float32 [2048], P('head'), may hold values from 0.25 to 1.75
- seg_ids: int32 [65536], P('ctx'), may hold values from 0 to 15, never falling along the last dimension, each value on 1 to 16384 neighbouring positions
Outputs:
- attended: bfloat16 [65536, 2048], P('ctx', 'head')
Inputs may be any that keep to these rules, and one draw needn't show every extreme that they name: `seg_ids`: segment numbers never fall along the stream; each segment covers 1 to 16384 consecutive tokens, and one covers exactly 16384.
All inputs are finite; a program needn't handle non-finite values.
Results may differ from a plain program's by a relative error of at most 0.012.
Values may be sent and summed in bfloat16 or wider, within the bound.
No kernel may reach another device: no remote copies, remote signals or barrier semaphores. Data moves between devices by JAX's collectives and lax.ppermute only.
A program may use at most 64 MiB of HBM per device.

v0:
```python
import jax
import jax.numpy as jnp
from jax import lax
from jax.sharding import PartitionSpec as P

HEAD_DIM = 128
SPAN = 16384


def shifted(value, axis, steps):
    count = lax.axis_size(axis)
    return lax.ppermute(value, axis, [(source, source + steps) for source in range(count - steps)])


def feature_map(values):
    return (jax.nn.elu(values.astype(jnp.float32)) + 1.0).astype(jnp.bfloat16)


def state_scan(kv_state, tail_id, row_count):
    head_count = kv_state.shape[0]
    flat = kv_state.reshape(head_count * HEAD_DIM, HEAD_DIM)
    tail_rows = jnp.full((8, HEAD_DIM), tail_id, jnp.float32)
    packed = jnp.concatenate([flat, tail_rows], axis=0)
    state_rows = head_count * HEAD_DIM
    is_state = (jnp.arange(packed.shape[0]) < state_rows)[:, None]
    count = lax.axis_size("ctx")
    window = min(count - 1, 1 + (SPAN - 1) // row_count)
    running = shifted(packed, "ctx", 1)
    step = 1
    while step < window:
        incoming = shifted(running, "ctx", step)
        linked = incoming[state_rows, 0] == running[state_rows, 0]
        running = running + jnp.where(is_state & linked, incoming, 0.0)
        step *= 2
    state_in = running[:state_rows].reshape(head_count, HEAD_DIM, HEAD_DIM)
    return (state_in, running[state_rows, 0])


def per_device(tokens, w_qkv, out_gain, seg_ids):
    whole = lax.all_gather(tokens, "head", axis=1, tiled=True)
    projected = jnp.einsum(
        "tr,grc->gtc",
        whole,
        lax.all_gather(w_qkv, "ctx", axis=1, tiled=True),
        preferred_element_type=jnp.float32,
    ).astype(jnp.bfloat16)
    row_count = seg_ids.shape[0]
    head_count = projected.shape[2] // HEAD_DIM
    queries = feature_map(projected[0]).reshape(row_count, head_count, HEAD_DIM)
    key_map = feature_map(projected[1]).reshape(row_count, head_count, HEAD_DIM)
    values = projected[2].reshape(row_count, head_count, HEAD_DIM)
    seg_float = seg_ids.astype(jnp.float32)
    tail_id = seg_float[-1]
    key_tail = jnp.where((seg_float == tail_id)[:, None, None], key_map, jnp.zeros_like(key_map))
    kv_state = jnp.einsum("thd,the->hde", key_tail, values, preferred_element_type=jnp.float32)
    state_in, tail_in = state_scan(kv_state, tail_id, row_count)
    block_rows = min(512, row_count)
    pieces = []
    for blk_no in range(row_count // block_rows):
        first_row = blk_no * block_rows
        key_end = first_row + block_rows
        query_blk = queries[first_row:key_end]
        query_pos = first_row + jnp.arange(block_rows, dtype=jnp.int32)
        query_seg = seg_float[first_row:key_end]
        scores = jnp.einsum(
            "bhd,shd->hbs", query_blk, key_map[:key_end], preferred_element_type=jnp.float32
        )
        visible = (jnp.arange(key_end, dtype=jnp.int32)[None, :] <= query_pos[:, None]) & (
            seg_float[None, :key_end] == query_seg[:, None]
        )
        weights = jnp.where(visible[None], scores, 0.0).astype(jnp.bfloat16)
        pieces.append(
            jnp.einsum(
                "hbs,she->bhe", weights, values[:key_end], preferred_element_type=jnp.float32
            )
        )
    local_part = jnp.concatenate(pieces, axis=0)
    state_low = state_in.astype(jnp.bfloat16)
    prefix = jnp.einsum("thd,hde->the", queries, state_low, preferred_element_type=jnp.float32)
    prefix = jnp.where((seg_float == tail_in)[:, None, None], prefix, 0.0)
    numerator = local_part + prefix
    inv_norm = lax.rsqrt(jnp.mean(numerator * numerator, axis=-1, keepdims=True) + 1e-05)
    result = numerator * inv_norm * out_gain.reshape(head_count, HEAD_DIM)
    return result.astype(jnp.bfloat16).reshape(row_count, head_count * HEAD_DIM)


def solution(mesh):
    placed = (P("ctx", "head"), P(None, "ctx", "head"), P("head"), P("ctx"))
    return jax.shard_map(
        per_device, mesh=mesh, in_specs=placed, out_specs=P("ctx", "head"), check_vma=False
    )
```

profile of v0, /device:TPU:32, one launch (start us, length us, event | category | flops | bytes accessed | tf_op | source)
XLA Modules:
  0.0 244.8 jit_solution(2544516807584703272)
XLA Ops:
  6.5 0.7 all-gather.3.cloned.1.call-update
  7.3 0.7 all-gather.5.cloned.1.call-update
  8.0 0.7 convert_element_type.60
  8.7 0.6 slice.88
  9.3 1.3 broadcast_compare_fusion.1
  10.6 0.2 fusion.25
  10.9 1.3 fusion.2
  12.2 84.3 %all-gather.3.cloned.1.call-done = bf16[3,2048,256]{2,1,0:T(8,128)(2,1)} async-done(((bf16[3,32,256]{2,1,0:T(8,128)(2,1)}), bf16[3,2048,256]{2,1,0:T(8,128)(2,1)}) %all-gather.3.cloned.1.call-update) | async-done | bytes 3145744 | tf_op jit(solution)/shard_map/all_gather | solution.py:44
  96.5 67.6 %all-gather.5.cloned.1.call-done = bf16[1024,2048]{1,0:T(8,128)(2,1)} async-done(((bf16[1024,256]{1,0:T(8,128)(2,1)}), bf16[1024,2048]{1,0:T(8,128)(2,1)}) %all-gather.5.cloned.1.call-update) | async-done | bytes 4194320 | tf_op jit(solution)/shard_map/all_gather | solution.py:40
  164.0 6.6 %fusion.7 = bf16[3,1024,256]{1,2,0:T(8,128)(2,1)S(1)} fusion(bf16[3,2048,256]{2,1,0:T(8,128)(2,1)} %all-gather.3.cloned.1.call-done, bf16[1024,2048]{1,0:T(8,128)(2,1)} %all-gather.5.cloned.1.call-done), kind=kOutput, calls=%fused_computation.16 | convolution fusion | flops 3222011904 | bytes 8912896 | tf_op jit(solution)/shard_map/tr,grc->gtc/dot_general | solution.py:41
  170.7 1.5 slice_convert_fusion.1
  172.2 1.3 copy.14
  173.5 2.1 fusion.31
  175.6 0.7 concatenate.7
  176.2 1.9 collective-permute-start
  178.2 0.5 fusion.17
  178.6 7.2 %collective-permute-done = f32[264,128]{1,0:T(8,128)S(1)} collective-permute-done((f32[264,128]{1,0:T(8,128)S(1)}, f32[264,128]{1,0:T(8,128)S(1)}, u32[]{:S(2)}, u32[]{:S(2)}) %collective-permute-start) | collective-permute-done | bytes 135200 | tf_op jit(solution)/shard_map/ppermute | solution.py:12
  185.9 1.9 collective-permute-start.1
  187.8 0.8 fusion.50
  188.6 0.6 slice.107
  189.2 6.3 %collective-permute-done.1 = f32[264,128]{1,0:T(8,128)S(1)} collective-permute-done((f32[264,128]{1,0:T(8,128)S(1)}, f32[264,128]{1,0:T(8,128)S(1)}, u32[]{:S(2)}, u32[]{:S(2)}) %collective-permute-start.1) | collective-permute-done | bytes 135200 | tf_op jit(solution)/shard_map/ppermute | solution.py:12
  195.5 0.5 slice.106
  197.2 0.1 select_add_fusion.3
  197.4 1.9 collective-permute-start.2
  199.3 3.9 %fusion.13 = f32[512,2,128]{0,2,1:T(8,128)} fusion(bf16[1024,2,128]{0,2,1:T(8,128)(2,1)S(1)} %bitcast.50, bf16[512,2,128]{0,2,1:T(8,128)(2,1)} %bitcast.54, pred[512,1024]{1,0:T(8,128)(4,1)} %fusion.2, f32[1024,2,128]{2,0,1:T(8,128)} %copy.14), kind=kOutput, calls=%fused_computation.21 | convolution fusion | flops 540278784 | bytes 2883584 | tf_op jit(solution)/shard_map/hbs,she->bhe/dot_general | solution.py:73
  203.2 0.7 slice.99
  203.9 0.3 copy.19
  204.2 0.6 slice.109
  204.8 2.9 %collective-permute-done.2 = f32[264,128]{1,0:T(8,128)} collective-permute-done((f32[264,128]{1,0:T(8,128)S(1)}, f32[264,128]{1,0:T(8,128)}, u32[]{:S(2)}, u32[]{:S(2)}) %collective-permute-start.2) | collective-permute-done | bytes 135200 | tf_op jit(solution)/shard_map/ppermute | solution.py:12
  207.7 1.2 slice.108
  210.2 1.0 select_add_fusion.2
  211.2 1.9 collective-permute-start.3
  213.1 0.2 fusion.30
  213.4 0.6 slice.111
  213.9 7.8 %collective-permute-done.3 = f32[264,128]{1,0:T(8,128)S(1)} collective-permute-done((f32[264,128]{1,0:T(8,128)S(1)}, f32[264,128]{1,0:T(8,128)S(1)}, u32[]{:S(2)}, u32[]{:S(2)}) %collective-permute-start.3) | collective-permute-done | bytes 135200 | tf_op jit(solution)/shard_map/ppermute | solution.py:12
  221.7 0.5 slice.110
  223.6 0.1 select_add_fusion.1
  223.7 1.9 collective-permute-start.4
  225.6 2.6 %fusion.14 = f32[512,2,128]{0,2,1:T(8,128)} fusion(bf16[512,2,128]{0,2,1:T(8,128)(2,1)} %bitcast.52, bf16[512,2,128]{0,2,1:T(8,128)(2,1)} %bitcast.53, bf16[512,2,128]{0,2,1:T(8,128)(2,1)S(1)} %bitcast.51, pred[512,512]{1,0:T(8,128)(4,1)S(1)} %fusion.25), kind=kOutput, calls=%fused_computation.22 | convolution fusion | flops 269484032 | bytes 1572864 | tf_op jit(solution)/shard_map/hbs,she->bhe/dot_general | solution.py:73
  228.2 0.6 slice.113
  228.8 3.0 %collective-permute-done.4 = f32[264,128]{1,0:T(8,128)S(1)} collective-permute-done((f32[264,128]{1,0:T(8,128)S(1)}, f32[264,128]{1,0:T(8,128)S(1)}, u32[]{:S(2)}, u32[]{:S(2)}) %collective-permute-start.4) | collective-permute-done | bytes 135200 | tf_op jit(solution)/shard_map/ppermute | solution.py:12
  231.8 0.5 slice.112
  233.6 0.1 select_add_fusion
  233.7 0.5 slice.114
  234.3 0.6 broadcast_compare_fusion
  234.9 1.8 multiply_reduce_fusion
  236.8 0.1 multiply_convert_fusion
  236.9 1.0 copy.23
  (20 shorter events, 0.1 us)
Async XLA Ops:
  6.5 89.9 %all-gather.3.cloned.1.call-start = ((), (), s32[]{:S(2)}) async-start(), calls=%async_computation | async-start | bytes 3194880 | tf_op jit(solution)/shard_map/all_gather | solution.py:44
  7.3 156.8 %all-gather.5.cloned.1.call-start = ((), (), s32[]{:S(2)}) async-start(), calls=%async_computation.1 | async-start | bytes 4718592 | tf_op jit(solution)/shard_map/all_gather | solution.py:40
  170.7 1.5 copy-start
  173.5 4.7 %copy-start.1 = (bf16[3,1024,256]{1,2,0:T(8,128)(2,1)S(1)}, bf16[3,1024,256]{1,2,0:T(8,128)(2,1)}, u32[]{:S(2)}) copy-start(bf16[3,1024,256]{1,2,0:T(8,128)(2,1)} %copy-done) | copy-start | bytes 4718596
  176.2 9.7 %collective-permute-start = (f32[264,128]{1,0:T(8,128)S(1)}, f32[264,128]{1,0:T(8,128)S(1)}, u32[]{:S(2)}, u32[]{:S(2)}) collective-permute-start(f32[264,128]{1,0:T(8,128)S(1)} %concatenate.7), channel_id=1, source_target_pairs={{0,8},{8,16},{16,24},{24,32},{32,40},{40,48},{48,56},{56,64},{64,7... | collective-permute-start | bytes 405512 | tf_op jit(solution)/shard_map/ppermute | solution.py:12
  185.9 9.6 %collective-permute-start.1 = (f32[264,128]{1,0:T(8,128)S(1)}, f32[264,128]{1,0:T(8,128)S(1)}, u32[]{:S(2)}, u32[]{:S(2)}) collective-permute-start(f32[264,128]{1,0:T(8,128)S(1)} %collective-permute-done), channel_id=1, source_target_pairs={{0,8},{8,16},{16,24},{24,32},{32,40},{40,48},{48,56},{56,64},{64,7... | collective-permute-start | bytes 405512 | tf_op jit(solution)/shard_map/ppermute | solution.py:12
  197.4 10.3 %collective-permute-start.2 = (f32[264,128]{1,0:T(8,128)S(1)}, f32[264,128]{1,0:T(8,128)}, u32[]{:S(2)}, u32[]{:S(2)}) collective-permute-start(f32[264,128]{1,0:T(8,128)S(1)} %select_add_fusion.3), channel_id=1, source_target_pairs={{0,16},{8,24},{16,32},{24,40},{32,48},{40,56},{48,64},{56,72},{64,... | collective-permute-start | bytes 405512 | tf_op jit(solution)/shard_map/ppermute | solution.py:12
  203.9 9.2 %copy-start.2 = (f32[1024,256]{0,1:T(8,128)S(1)}, f32[1024,256]{0,1:T(8,128)}, u32[]{:S(2)}) copy-start(f32[1024,256]{0,1:T(8,128)} %get-tuple-element.6) | copy-start | bytes 3145732
  211.2 23.1 %copy-start.3 = (s32[1024]{0:T(1024)S(1)}, s32[1024]{0:T(1024)}, u32[]{:S(2)}) copy-start(s32[1024]{0:T(1024)} %param.7) | copy-start | bytes 12292
  211.2 10.5 %collective-permute-start.3 = (f32[264,128]{1,0:T(8,128)S(1)}, f32[264,128]{1,0:T(8,128)S(1)}, u32[]{:S(2)}, u32[]{:S(2)}) collective-permute-start(f32[264,128]{1,0:T(8,128)S(1)} %select_add_fusion.2), channel_id=1, source_target_pairs={{0,32},{8,40},{16,48},{24,56},{32,64},{40,72},{48,80},{56,88},{64,... | collective-permute-start | bytes 405512 | tf_op jit(solution)/shard_map/ppermute | solution.py:12
  223.7 8.1 %collective-permute-start.4 = (f32[264,128]{1,0:T(8,128)S(1)}, f32[264,128]{1,0:T(8,128)S(1)}, u32[]{:S(2)}, u32[]{:S(2)}) collective-permute-start(f32[264,128]{1,0:T(8,128)S(1)} %select_add_fusion.1), channel_id=1, source_target_pairs={{0,64},{8,72},{16,80},{24,88},{32,96},{40,104},{48,112},{56,120},{... | collective-permute-start | bytes 405512 | tf_op jit(solution)/shard_map/ppermute | solution.py:12
  233.6 3.2 %copy-start.4 = (f32[256]{0:T(256)S(1)}, f32[256]{0:T(256)}, u32[]{:S(2)}) copy-start(f32[256]{0:T(256)} %param.6) | copy-start | bytes 3076
Sparse Core Ops, SparseCore 0:
  10.8 85.6 all-gather.2
  98.5 65.5 all-gather.4
where the time goes:
time: 245 us
  waiting for transfers between devices  180 us (73%)
  between operations  18.7 us (8%)
  matrix products  17 us (7%)
  local copies, waits for them, and re-layouts  11.1 us (5%)
  starting transfers between devices  9.63 us (4%)
  other arithmetic  7.82 us (3%)
    all_gather x1, waiting for transfers between devices, per_device(): lax.all_gather(w_qkv, 'ctx', axis=1, tiled=True)  84.3 us
    all_gather x1, waiting for transfers between devices, per_device(): whole = lax.all_gather(tokens, 'head', axis=1, tiled=True)  67.6 us
    ppermute x5, waiting for transfers between devices, shifted(): lax.ppermute(value, axis, [(source, source + steps) for source in range(c...  27.2 us
    ppermute x5, starting transfers between devices, shifted(): lax.ppermute(value, axis, [(source, source + steps) for source in range(c...  9.59 us
    dot_general x1, matrix products, per_device(): jnp.einsum('tr,grc->gtc', whole, lax.all_gather(w_qkv, 'ctx', axis=1, til...  6.6 us
    dot_general x2, matrix products, per_device(): jnp.einsum('hbs,she->bhe', weights, values[:key_end], preferred_element_t...  6.48 us
    slice x8, local copies, waits for them, and re-layouts, state_scan(): linked = incoming[state_rows, 0] == running[state_rows, 0]  5.04 us
  transfers between devices with their start and end apart: 7, of which 7 were waited for; matrix products, arithmetic and copies ran while one was open for 6% of the time, Pallas kernels for 0%

commit v1 on v0

--- a/solution.py
+++ b/solution.py
@@ -37,7 +37,12 @@
 
 
 def per_device(tokens, w_qkv, out_gain, seg_ids):
-    whole = lax.all_gather(tokens, "head", axis=1, tiled=True)
+    ring = [tokens]
+    for hop in range(7):
+        ring.append(lax.ppermute(ring[-1], "head", [(dev, (dev + 1) % 8) for dev in range(8)]))
+    whole = jnp.roll(
+        jnp.concatenate(ring[::-1], axis=1), (lax.axis_index("head") + 1) * ring[0].shape[1], axis=1
+    )
     projected = jnp.einsum(
         "tr,grc->gtc",
         whole,

time: 245 us -> 215 us (0.88)
  waiting for transfers between devices: 180 us -> 115 us
  local copies, waits for them, and re-layouts: 11.1 us -> 31.2 us
  starting transfers between devices: 9.63 us -> 25.3 us
    ppermute x0 -> x7, waiting for transfers between devices: none -> 87.6 us  [per_device(): lax.ppermute(ring[-1], 'head', [(dev, (dev + 1) % 8) for dev in range(8)])]
    all_gather x1, waiting for transfers between devices: 84.3 us -> 0.01 us  [per_device(): lax.all_gather(w_qkv, 'ctx', axis=1, tiled=True)]
    all_gather x1 -> x0, waiting for transfers between devices: 67.6 us -> none  [per_device(): whole = lax.all_gather(tokens, 'head', axis=1, tiled=True)]
    unnamed x10 -> x23, local copies, waits for them, and re-layouts: 0.02 us -> 18.6 us
    ppermute x0 -> x7, starting transfers between devices: none -> 15.7 us  [per_device(): lax.ppermute(ring[-1], 'head', [(dev, (dev + 1) % 8) for dev in range(8)])]
  transfers between devices with their start and end apart: 7 -> 13, of which waited for: 7 -> 12; matrix products, arithmetic and copies ran while one was open for 6% -> 16% of each run, Pallas kernels for 0% -> 0%
where the time goes in v1:
time: 215 us; the launch traced here: 214 us
  waiting for transfers between devices  115 us (53%)
  local copies, waits for them, and re-layouts  31.2 us (15%)
  starting transfers between devices  25.3 us (12%)
  between operations  18.5 us (9%)
  matrix products  16.2 us (8%)
  other arithmetic  8.54 us (4%)
    ppermute x7, waiting for transfers between devices, per_device(): lax.ppermute(ring[-1], 'head', [(dev, (dev + 1) % 8) for dev in range(8)])  87.6 us
    ppermute x5, waiting for transfers between devices, shifted(): lax.ppermute(value, axis, [(source, source + steps) for source in range(c...  26.3 us
    unnamed x23, local copies, waits for them, and re-layouts  18.6 us
    ppermute x7, starting transfers between devices, per_device(): lax.ppermute(ring[-1], 'head', [(dev, (dev + 1) % 8) for dev in range(8)])  15.7 us
    ppermute x5, starting transfers between devices, shifted(): lax.ppermute(value, axis, [(source, source + steps) for source in range(c...  9.59 us
    dot_general x1, matrix products, per_device(): jnp.einsum('tr,grc->gtc', whole, lax.all_gather(w_qkv, 'ctx', axis=1, til...  6.63 us
    dot_general x2, matrix products, per_device(): jnp.einsum('hbs,she->bhe', weights, values[:key_end], preferred_element_t...  5.77 us
    slice x8, local copies, waits for them, and re-layouts, state_scan(): linked = incoming[state_rows, 0] == running[state_rows, 0]  4.8 us
  transfers between devices with their start and end apart: 13, of which 12 were waited for; matrix products, arithmetic and copies ran while one was open for 16% of the time, Pallas kernels for 0%

profile of v1, /device:TPU:32, one launch (start us, length us, event | category | flops | bytes accessed | tf_op | source)
XLA Modules:
  0.0 214.4 jit_solution(4647401746939299892)
XLA Ops:
  7.3 4.3 %collective-permute-start = (bf16[1024,256]{1,0:T(8,128)(2,1)}, bf16[1024,256]{1,0:T(8,128)(2,1)S(1)}, u32[]{:S(2)}, u32[]{:S(2)}) collective-permute-start(bf16[1024,256]{1,0:T(8,128)(2,1)} %param.4), channel_id=1, source_target_pairs={{0,1},{1,2},{2,3},{3,4},{4,5},{5,6},{6,7},{7,0},{8,9},{9,10},{10,1... | collective-permute-start | bytes 1572872 | tf_op jit(solution)/shard_map/ppermute | solution.py:42
  11.5 18.8 %collective-permute-done = bf16[1024,256]{1,0:T(8,128)(2,1)S(1)} collective-permute-done((bf16[1024,256]{1,0:T(8,128)(2,1)}, bf16[1024,256]{1,0:T(8,128)(2,1)S(1)}, u32[]{:S(2)}, u32[]{:S(2)}) %collective-permute-start) | collective-permute-done | bytes 524320 | tf_op jit(solution)/shard_map/ppermute | solution.py:42
  30.3 1.9 collective-permute-start.1
  32.2 14.3 %collective-permute-done.1 = bf16[1024,256]{1,0:T(8,128)(2,1)S(1)} collective-permute-done((bf16[1024,256]{1,0:T(8,128)(2,1)S(1)}, bf16[1024,256]{1,0:T(8,128)(2,1)S(1)}, u32[]{:S(2)}, u32[]{:S(2)}) %collective-permute-start.1) | collective-permute-done | bytes 524320 | tf_op jit(solution)/shard_map/ppermute | solution.py:42
  46.5 1.9 collective-permute-start.2
  48.5 13.4 %collective-permute-done.2 = bf16[1024,256]{1,0:T(8,128)(2,1)S(1)} collective-permute-done((bf16[1024,256]{1,0:T(8,128)(2,1)S(1)}, bf16[1024,256]{1,0:T(8,128)(2,1)S(1)}, u32[]{:S(2)}, u32[]{:S(2)}) %collective-permute-start.2) | collective-permute-done | bytes 524320 | tf_op jit(solution)/shard_map/ppermute | solution.py:42
  61.8 1.9 collective-permute-start.3
  63.7 12.4 %collective-permute-done.3 = bf16[1024,256]{1,0:T(8,128)(2,1)S(1)} collective-permute-done((bf16[1024,256]{1,0:T(8,128)(2,1)S(1)}, bf16[1024,256]{1,0:T(8,128)(2,1)S(1)}, u32[]{:S(2)}, u32[]{:S(2)}) %collective-permute-start.3) | collective-permute-done | bytes 524320 | tf_op jit(solution)/shard_map/ppermute | solution.py:42
  76.2 1.9 collective-permute-start.4
  78.1 11.5 %collective-permute-done.4 = bf16[1024,256]{1,0:T(8,128)(2,1)S(1)} collective-permute-done((bf16[1024,256]{1,0:T(8,128)(2,1)S(1)}, bf16[1024,256]{1,0:T(8,128)(2,1)S(1)}, u32[]{:S(2)}, u32[]{:S(2)}) %collective-permute-start.4) | collective-permute-done | bytes 524320 | tf_op jit(solution)/shard_map/ppermute | solution.py:42
  89.6 1.9 collective-permute-start.5
  92.9 1.4 broadcast_compare_fusion.1
  94.2 8.1 %collective-permute-done.5 = bf16[1024,256]{1,0:T(8,128)(2,1)} collective-permute-done((bf16[1024,256]{1,0:T(8,128)(2,1)S(1)}, bf16[1024,256]{1,0:T(8,128)(2,1)}, u32[]{:S(2)}, u32[]{:S(2)}) %collective-permute-start.5) | collective-permute-done | bytes 524320 | tf_op jit(solution)/shard_map/ppermute | solution.py:42
  102.3 1.9 collective-permute-start.6
  104.5 1.3 fusion.3
  105.8 9.1 %collective-permute-done.6 = bf16[1024,256]{1,0:T(8,128)(2,1)} collective-permute-done((bf16[1024,256]{1,0:T(8,128)(2,1)}, bf16[1024,256]{1,0:T(8,128)(2,1)}, u32[]{:S(2)}, u32[]{:S(2)}) %collective-permute-start.6) | collective-permute-done | bytes 524320 | tf_op jit(solution)/shard_map/ppermute | solution.py:42
  114.9 1.9 constant_dynamic-update-slice_fusion.15
  116.8 1.9 constant_dynamic-update-slice_fusion.14
  118.8 0.9 constant_dynamic-update-slice_fusion.13
  119.7 0.9 constant_dynamic-update-slice_fusion.12
  120.6 0.9 constant_dynamic-update-slice_fusion.11
  124.1 1.9 constant_dynamic-update-slice_fusion.7
  126.0 1.9 constant_dynamic-update-slice_fusion.6
  127.9 0.9 constant_dynamic-update-slice_fusion.5
  132.4 0.9 constant_dynamic-update-slice_fusion
  133.3 6.6 %fusion.8 = bf16[3,1024,256]{1,2,0:T(8,128)(2,1)S(1)} fusion(bf16[3,2048,256]{2,1,0:T(8,128)(2,1)} %all-gather.2.cloned.1.call-done, bf16[1024,4096]{1,0:T(8,128)(2,1)} %constant_dynamic-update-slice_fusion, s32[]{:T(128)S(6)} %select_n.74), kind=kOutput, calls=%fused_computation.17 | convolution fusion | flops 3222011904 | bytes 8912900 | tf_op jit(solution)/shard_map/tr,grc->gtc/dot_general | solution.py:46
  139.9 1.2 copy-done
  141.1 1.1 slice_convert_fusion.1
  142.2 1.3 copy.14
  143.5 2.1 fusion.32
  146.4 1.9 collective-permute-start.7
  148.3 1.5 fusion.18
  149.8 6.2 %collective-permute-done.7 = f32[264,128]{1,0:T(8,128)S(1)} collective-permute-done((f32[264,128]{1,0:T(8,128)S(1)}, f32[264,128]{1,0:T(8,128)S(1)}, u32[]{:S(2)}, u32[]{:S(2)}) %collective-permute-start.7) | collective-permute-done | bytes 135200 | tf_op jit(solution)/shard_map/ppermute | solution.py:12
  156.0 1.9 collective-permute-start.8
  159.1 6.5 %collective-permute-done.8 = f32[264,128]{1,0:T(8,128)S(1)} collective-permute-done((f32[264,128]{1,0:T(8,128)S(1)}, f32[264,128]{1,0:T(8,128)S(1)}, u32[]{:S(2)}, u32[]{:S(2)}) %collective-permute-start.8) | collective-permute-done | bytes 135200 | tf_op jit(solution)/shard_map/ppermute | solution.py:12
  167.5 1.9 collective-permute-start.9
  169.4 4.0 %fusion.14 = f32[512,2,128]{0,2,1:T(8,128)} fusion(bf16[1024,2,128]{0,2,1:T(8,128)(2,1)} %bitcast.50, bf16[512,2,128]{0,2,1:T(8,128)(2,1)S(1)} %bitcast.54, pred[512,1024]{1,0:T(8,128)(4,1)} %fusion.3, f32[1024,2,128]{2,0,1:T(8,128)} %copy.14), kind=kOutput, calls=%fused_computation.22 | convolution fusion | flops 540278784 | bytes 2883584 | tf_op jit(solution)/shard_map/hbs,she->bhe/dot_general | solution.py:78
  173.4 1.7 slice.99
  175.9 1.9 collective-permute-done.9
  177.8 1.2 slice.108
  180.2 1.0 select_add_fusion.2
  181.2 1.9 collective-permute-start.10
  183.9 7.8 %collective-permute-done.10 = f32[264,128]{1,0:T(8,128)S(1)} collective-permute-done((f32[264,128]{1,0:T(8,128)S(1)}, f32[264,128]{1,0:T(8,128)S(1)}, u32[]{:S(2)}, u32[]{:S(2)}) %collective-permute-start.10) | collective-permute-done | bytes 135200 | tf_op jit(solution)/shard_map/ppermute | solution.py:12
  193.6 1.9 collective-permute-start.11
  195.5 1.8 fusion.15
  197.8 3.9 %collective-permute-done.11 = f32[264,128]{1,0:T(8,128)S(1)} collective-permute-done((f32[264,128]{1,0:T(8,128)S(1)}, f32[264,128]{1,0:T(8,128)S(1)}, u32[]{:S(2)}, u32[]{:S(2)}) %collective-permute-start.11) | collective-permute-done | bytes 135200 | tf_op jit(solution)/shard_map/ppermute | solution.py:12
  204.7 1.7 multiply_reduce_fusion
  206.6 1.0 copy.23
  (45 shorter events, 15.7 us)
Async XLA Ops:
  6.5 116.7 %copy-start.1 = (bf16[1024,256]{1,0:T(8,128)(2,1)S(1)}, bf16[1024,256]{1,0:T(8,128)(2,1)}, u32[]{:S(2)}) copy-start(bf16[1024,256]{1,0:T(8,128)(2,1)} %param.4) | copy-start | bytes 1572868
  6.5 126.7 %all-gather.2.cloned.1.call-start = ((), (), s32[]{:S(2)}) async-start(), calls=%async_computation | async-start | bytes 3194880 | tf_op jit(solution)/shard_map/all_gather | solution.py:49
  7.3 23.1 %collective-permute-start = (bf16[1024,256]{1,0:T(8,128)(2,1)}, bf16[1024,256]{1,0:T(8,128)(2,1)S(1)}, u32[]{:S(2)}, u32[]{:S(2)}) collective-permute-start(bf16[1024,256]{1,0:T(8,128)(2,1)} %param.4), channel_id=1, source_target_pairs={{0,1},{1,2},{2,3},{3,4},{4,5},{5,6},{6,7},{7,0},{8,9},{9,10},{10,1... | collective-permute-start | bytes 1572872 | tf_op jit(solution)/shard_map/ppermute | solution.py:42
  30.3 16.2 %collective-permute-start.1 = (bf16[1024,256]{1,0:T(8,128)(2,1)S(1)}, bf16[1024,256]{1,0:T(8,128)(2,1)S(1)}, u32[]{:S(2)}, u32[]{:S(2)}) collective-permute-start(bf16[1024,256]{1,0:T(8,128)(2,1)S(1)} %collective-permute-done), channel_id=1, source_target_pairs={{0,1},{1,2},{2,3},{3,4},{4,5},{5,6},{6,7},{7,0},{8,9},{9,10},{10,1... | collective-permute-start | bytes 1572872 | tf_op jit(solution)/shard_map/ppermute | solution.py:42
  46.5 15.3 %collective-permute-start.2 = (bf16[1024,256]{1,0:T(8,128)(2,1)S(1)}, bf16[1024,256]{1,0:T(8,128)(2,1)S(1)}, u32[]{:S(2)}, u32[]{:S(2)}) collective-permute-start(bf16[1024,256]{1,0:T(8,128)(2,1)S(1)} %collective-permute-done.1), channel_id=1, source_target_pairs={{0,1},{1,2},{2,3},{3,4},{4,5},{5,6},{6,7},{7,0},{8,9},{9,10},{10,1... | collective-permute-start | bytes 1572872 | tf_op jit(solution)/shard_map/ppermute | solution.py:42
  61.8 14.4 %collective-permute-start.3 = (bf16[1024,256]{1,0:T(8,128)(2,1)S(1)}, bf16[1024,256]{1,0:T(8,128)(2,1)S(1)}, u32[]{:S(2)}, u32[]{:S(2)}) collective-permute-start(bf16[1024,256]{1,0:T(8,128)(2,1)S(1)} %collective-permute-done.2), channel_id=1, source_target_pairs={{0,1},{1,2},{2,3},{3,4},{4,5},{5,6},{6,7},{7,0},{8,9},{9,10},{10,1... | collective-permute-start | bytes 1572872 | tf_op jit(solution)/shard_map/ppermute | solution.py:42
  76.2 13.4 %collective-permute-start.4 = (bf16[1024,256]{1,0:T(8,128)(2,1)S(1)}, bf16[1024,256]{1,0:T(8,128)(2,1)S(1)}, u32[]{:S(2)}, u32[]{:S(2)}) collective-permute-start(bf16[1024,256]{1,0:T(8,128)(2,1)S(1)} %collective-permute-done.3), channel_id=1, source_target_pairs={{0,1},{1,2},{2,3},{3,4},{4,5},{5,6},{6,7},{7,0},{8,9},{9,10},{10,1... | collective-permute-start | bytes 1572872 | tf_op jit(solution)/shard_map/ppermute | solution.py:42
  89.6 12.7 %collective-permute-start.5 = (bf16[1024,256]{1,0:T(8,128)(2,1)S(1)}, bf16[1024,256]{1,0:T(8,128)(2,1)}, u32[]{:S(2)}, u32[]{:S(2)}) collective-permute-start(bf16[1024,256]{1,0:T(8,128)(2,1)S(1)} %collective-permute-done.4), channel_id=1, source_target_pairs={{0,1},{1,2},{2,3},{3,4},{4,5},{5,6},{6,7},{7,0},{8,9},{9,10},{10,1... | collective-permute-start | bytes 1572872 | tf_op jit(solution)/shard_map/ppermute | solution.py:42
  102.3 12.6 %collective-permute-start.6 = (bf16[1024,256]{1,0:T(8,128)(2,1)}, bf16[1024,256]{1,0:T(8,128)(2,1)}, u32[]{:S(2)}, u32[]{:S(2)}) collective-permute-start(bf16[1024,256]{1,0:T(8,128)(2,1)} %collective-permute-done.5), channel_id=1, source_target_pairs={{0,1},{1,2},{2,3},{3,4},{4,5},{5,6},{6,7},{7,0},{8,9},{9,10},{10,1... | collective-permute-start | bytes 1572872 | tf_op jit(solution)/shard_map/ppermute | solution.py:42
  139.9 1.2 copy-start
  145.6 58.4 %copy-start.2 = (s32[1024]{0:T(1024)S(1)}, s32[1024]{0:T(1024)}, u32[]{:S(2)}) copy-start(s32[1024]{0:T(1024)} %param.7) | copy-start | bytes 12292
  146.4 9.7 %collective-permute-start.7 = (f32[264,128]{1,0:T(8,128)S(1)}, f32[264,128]{1,0:T(8,128)S(1)}, u32[]{:S(2)}, u32[]{:S(2)}) collective-permute-start(f32[264,128]{1,0:T(8,128)S(1)} %concatenate.14), channel_id=1, source_target_pairs={{0,8},{8,16},{16,24},{24,32},{32,40},{40,48},{48,56},{56,64},{64,7... | collective-permute-start | bytes 405512 | tf_op jit(solution)/shard_map/ppermute | solution.py:12
  156.0 9.6 %collective-permute-start.8 = (f32[264,128]{1,0:T(8,128)S(1)}, f32[264,128]{1,0:T(8,128)S(1)}, u32[]{:S(2)}, u32[]{:S(2)}) collective-permute-start(f32[264,128]{1,0:T(8,128)S(1)} %collective-permute-done.7), channel_id=1, source_target_pairs={{0,8},{8,16},{16,24},{24,32},{32,40},{40,48},{48,56},{56,64},{64,7... | collective-permute-start | bytes 405512 | tf_op jit(solution)/shard_map/ppermute | solution.py:12
  167.5 10.3 %collective-permute-start.9 = (f32[264,128]{1,0:T(8,128)S(1)}, f32[264,128]{1,0:T(8,128)}, u32[]{:S(2)}, u32[]{:S(2)}) collective-permute-start(f32[264,128]{1,0:T(8,128)S(1)} %select_add_fusion.3), channel_id=1, source_target_pairs={{0,16},{8,24},{16,32},{24,40},{32,48},{40,56},{48,64},{56,72},{64,... | collective-permute-start | bytes 405512 | tf_op jit(solution)/shard_map/ppermute | solution.py:12
  169.4 37.0 %copy-start.3 = (f32[256]{0:T(256)S(1)}, f32[256]{0:T(256)}, u32[]{:S(2)}) copy-start(f32[256]{0:T(256)} %param.6) | copy-start | bytes 3076
  181.2 10.5 %collective-permute-start.10 = (f32[264,128]{1,0:T(8,128)S(1)}, f32[264,128]{1,0:T(8,128)S(1)}, u32[]{:S(2)}, u32[]{:S(2)}) collective-permute-start(f32[264,128]{1,0:T(8,128)S(1)} %select_add_fusion.2), channel_id=1, source_target_pairs={{0,32},{8,40},{16,48},{24,56},{32,64},{40,72},{48,80},{56,88},{64,... | collective-permute-start | bytes 405512 | tf_op jit(solution)/shard_map/ppermute | solution.py:12
  193.6 8.1 %collective-permute-start.11 = (f32[264,128]{1,0:T(8,128)S(1)}, f32[264,128]{1,0:T(8,128)S(1)}, u32[]{:S(2)}, u32[]{:S(2)}) collective-permute-start(f32[264,128]{1,0:T(8,128)S(1)} %select_add_fusion.1), channel_id=1, source_target_pairs={{0,64},{8,72},{16,80},{24,88},{32,96},{40,104},{48,112},{56,120},{... | collective-permute-start | bytes 405512 | tf_op jit(solution)/shard_map/ppermute | solution.py:12
Sparse Core Ops, SparseCore 0:
  10.8 85.6 all-gather.1
